TPU v7x, 32 devices: a whole 2x2x4 slice. The times are simulated.
32 devices in a mesh: seq: 4 (over y, x), exp: 8 (over z, core).
Axes of the slice: x: 2, y: 2, z: 4, core: 2. Of those that a mesh axis runs over, the one named last changes fastest.
Arguments:
- token_ids: int32 [4, 32], replicated, may hold values from 0 to 51199
- cache_lengths: int32 [32], replicated, may hold values from 1 to 1024, as said below
- empty_blocks: int32 [32, 64], replicated, may hold values 0 or 1
- expert_ids: int32 [4, 32, 6], replicated, may hold values from 0 to 63, all different within a row
- embed_table: bfloat16 [51200, 2048], P(('seq', 'exp')), may hold values from -3 to 3
- attn_gain: float32 [2048], replicated, may hold values from 0.5 to 1.5
- w_query: bfloat16 [2048, 2048], P(None, 'seq'), may hold values from -0.125 to 0.125
- w_key: bfloat16 [2048, 2048], P(None, 'seq'), may hold values from -0.125 to 0.125
- w_value: bfloat16 [2048, 2048], P(None, 'seq'), may hold values from -0.125 to 0.125
- w_out: bfloat16 [2048, 2048], P('seq'), may hold values from -0.125 to 0.125
- k_cache: bfloat16 [32, 1024, 2048], P('exp', 'seq'), may hold values from -200 to 200
- v_cache: bfloat16 [32, 1024, 2048], P('exp', 'seq'), may hold values from -6 to 6
- moe_gain: float32 [2048], replicated, may hold values from 0.5 to 1.5
- w_router: bfloat16 [2048, 64], replicated, may hold values from -0.125 to 0.125
- gate_pieces: bfloat16 [256, 2048, 352], P(('seq', 'exp')), may hold values from -0.125 to 0.125
- up_pieces: bfloat16 [256, 2048, 352], P(('seq', 'exp')), may hold values from -0.125 to 0.125
- down_pieces: bfloat16 [256, 352, 2048], P(('seq', 'exp')), may hold values from -0.15625 to 0.15625
- shared_gate: bfloat16 [2048, 2816], P(None, 'exp'), may hold values from -0.125 to 0.125
- shared_up: bfloat16 [2048, 2816], P(None, 'exp'), may hold values from -0.125 to 0.125
- shared_down: bfloat16 [2816, 2048], P('exp'), may hold values from -0.109375 to 0.109375
- final_gain: float32 [2048], replicated, may hold values from 0.5 to 1.5
- w_head: bfloat16 [2048, 51200], P(None, ('seq', 'exp')), may hold values from -0.125 to 0.125
Outputs:
- hidden_norms: float32 [4, 32], replicated
- greatest_logits: float32 [4, 32], replicated
Inputs may be any that keep to these rules, and one draw needn't show every extreme that they name: `cache_lengths`: one of the 32 requests has exactly 1024 cached positions in every draw.
All inputs are finite; a program needn't handle non-finite values.
Results may differ from a plain program's by a relative error of at most 0.0055.
Values may be sent and summed in bfloat16 or wider, within the bound.
No kernel may reach another device: no remote copies, remote signals or barrier semaphores. Data moves between devices by JAX's collectives and lax.ppermute only.
A program may use at most 128 MiB of HBM per device.

v0:
```python
import math
import jax
import jax.numpy as jnp
from jax import lax
from jax.sharding import PartitionSpec as P

HDIM = 128
PIECES = 4
BLK = 16
epsilon = 1e-06
negative = -1e30


def rms_scale(values, scales):
    return values * lax.rsqrt(jnp.mean(values * values, axis=-1, keepdims=True) + epsilon) * scales


def rotate(values, places):
    half_width = values.shape[-1] // 2
    frequency = 10000.0 ** (-2.0 * jnp.arange(half_width, dtype=jnp.float32) / values.shape[-1])
    angles = places.astype(jnp.float32)[..., None, None] * frequency
    cosine_table = jnp.cos(angles)
    sine_table = jnp.sin(angles)
    lower = values[..., :half_width]
    upper = values[..., half_width:]
    return jnp.concatenate(
        [lower * cosine_table - upper * sine_table, upper * cosine_table + lower * sine_table],
        axis=-1,
    )


def gather_all(values):
    inner = lax.all_gather(values, "exp", axis=0, tiled=False)
    return lax.all_gather(inner, "seq", axis=0, tiled=False)


def on_device(
    token_ids,
    cache_lengths,
    empty_blocks,
    expert_ids,
    embed_table,
    attn_gain,
    w_query,
    w_key,
    w_value,
    w_out,
    k_cache,
    v_cache,
    moe_gain,
    w_router,
    gate_pieces,
    up_pieces,
    down_pieces,
    shared_gate,
    shared_up,
    shared_down,
    final_gain,
    w_head,
):
    steps, requests = token_ids.shape
    tokens = steps * requests
    width = embed_table.shape[1]
    vocab_local = embed_table.shape[0]
    n_seq = lax.axis_size("seq")
    n_exp = lax.axis_size("exp")
    n_dev = n_seq * n_exp
    owner_index = lax.axis_index(("seq", "exp"))
    seq_index = lax.axis_index("seq")
    own_count = requests // n_exp
    own_start = lax.axis_index("exp") * own_count
    group = steps * own_count
    share = group // n_seq

    def grouped(values):
        rest = values.shape[2:]
        by_group = jnp.moveaxis(values.reshape((steps, n_exp, own_count) + rest), 1, 0)
        return by_group.reshape((tokens,) + rest)

    def natural(values):
        split = jnp.swapaxes(values.reshape(n_seq, n_exp, share), 0, 1)
        grouped = split.reshape(n_exp, steps, own_count)
        return jnp.moveaxis(grouped, 0, 1).reshape(steps, requests)

    group_ids = jnp.moveaxis(token_ids.reshape(steps, n_exp, own_count), 1, 0)
    local_ids = group_ids - owner_index * vocab_local
    held = (local_ids >= 0) & (local_ids < vocab_local)
    rows = jnp.take(embed_table, jnp.clip(local_ids, 0, vocab_local - 1), axis=0)
    rows = jnp.where(held[..., None], rows, jnp.zeros((), rows.dtype))
    arrived = lax.all_to_all(rows, "exp", 0, 0, tiled=True)
    row_part = jnp.sum(arrived.astype(jnp.float32), axis=0).astype(jnp.bfloat16)
    row_parts = lax.all_gather(row_part, "seq", axis=0, tiled=False)
    embedded = jnp.sum(row_parts.astype(jnp.float32), axis=0).reshape(group, width)
    attn_in = rms_scale(embedded, attn_gain).astype(jnp.bfloat16)
    own_lengths = lax.dynamic_slice_in_dim(cache_lengths, own_start, own_count, 0)
    places = (own_lengths[None, :] + jnp.arange(steps, dtype=jnp.int32)[:, None]).reshape(group)
    heads_here = w_query.shape[1] // HDIM

    def project(weight):
        return jnp.dot(attn_in, weight, preferred_element_type=jnp.float32).reshape(
            group, heads_here, HDIM
        )

    query_part = rotate(project(w_query), places).astype(jnp.bfloat16)
    key_part = rotate(project(w_key), places).astype(jnp.bfloat16)
    value_part = project(w_value).astype(jnp.bfloat16)
    every = lax.all_gather(
        jnp.stack([query_part, key_part, value_part], axis=0), "seq", axis=0, tiled=False
    )
    head_count = n_seq * heads_here
    every = jnp.moveaxis(every, 0, 2).reshape(3, steps, own_count, head_count, HDIM)
    queries = every[0]
    span = k_cache.shape[1]
    first_place = seq_index * span
    places_here = first_place + jnp.arange(span, dtype=jnp.int32)
    own_empty = lax.dynamic_slice_in_dim(empty_blocks, own_start, own_count, 0)
    local_blocks = lax.dynamic_slice_in_dim(own_empty, first_place // BLK, span // BLK, 1)
    blocked = jnp.broadcast_to(local_blocks[:, :, None], (own_count, span // BLK, BLK)).reshape(
        own_count, span
    )
    live_mask = ((places_here[None, :] < own_lengths[:, None]) & (blocked == 0))[None, :, None, :]
    cache_keys = k_cache.reshape(own_count, span, head_count, HDIM)
    cache_values = v_cache.reshape(own_count, span, head_count, HDIM)
    score_scale = 1.0 / math.sqrt(HDIM)
    cached = (
        jnp.einsum("trhd,rphd->trhp", queries, cache_keys, preferred_element_type=jnp.float32)
        * score_scale
    )
    local_top = jnp.max(jnp.where(live_mask, cached, negative), axis=3)
    local_weights = jnp.where(live_mask, jnp.exp(cached - local_top[..., None]), 0.0)
    local_totals = jnp.sum(local_weights, axis=3)
    local_mixture = jnp.einsum(
        "trhp,rphd->trhd",
        local_weights.astype(jnp.bfloat16),
        cache_values,
        preferred_element_type=jnp.float32,
    )

    def by_owner(values):
        rest = values.shape[3:]
        split = values.reshape((steps, own_count, n_seq, heads_here) + rest)
        return jnp.moveaxis(split, 2, 0).reshape(n_seq, -1)

    mix_len = group * heads_here * HDIM
    stat_len = group * heads_here
    packed = jnp.concatenate(
        [by_owner(local_mixture), by_owner(local_top), by_owner(local_totals)], axis=1
    )
    got = lax.all_to_all(packed, "seq", 0, 0, tiled=True)
    got_mixture = got[:, :mix_len].reshape(n_seq, steps, own_count, heads_here, HDIM)
    got_top = got[:, mix_len : mix_len + stat_len].reshape(n_seq, steps, own_count, heads_here)
    got_totals = got[:, mix_len + stat_len :].reshape(n_seq, steps, own_count, heads_here)
    own_queries = query_part.reshape(steps, own_count, heads_here, HDIM)
    own_keys = key_part.reshape(steps, own_count, heads_here, HDIM)
    own_values = value_part.reshape(steps, own_count, heads_here, HDIM)
    fresh_scores = (
        jnp.einsum("trhd,urhd->trhu", own_queries, own_keys, preferred_element_type=jnp.float32)
        * score_scale
    )
    causal = (jnp.arange(steps)[None, :] <= jnp.arange(steps)[:, None])[:, None, None, :]
    fresh_top = jnp.max(jnp.where(causal, fresh_scores, negative), axis=3)
    fresh_weights = jnp.where(causal, jnp.exp(fresh_scores - fresh_top[..., None]), 0.0)
    fresh_mixture = jnp.einsum(
        "trhu,urhd->trhd",
        fresh_weights.astype(jnp.bfloat16),
        own_values,
        preferred_element_type=jnp.float32,
    )
    top_score = jnp.maximum(jnp.max(got_top, axis=0), fresh_top)
    cache_factor = jnp.exp(got_top - top_score[None])
    fresh_factor = jnp.exp(fresh_top - top_score)
    totals = (
        jnp.sum(got_totals * cache_factor, axis=0) + jnp.sum(fresh_weights, axis=3) * fresh_factor
    )
    mixture = (
        jnp.sum(got_mixture * cache_factor[..., None], axis=0)
        + fresh_mixture * fresh_factor[..., None]
    )
    own_heads = (mixture / totals[..., None]).astype(jnp.bfloat16).reshape(group, heads_here * HDIM)
    attn_part = jnp.dot(own_heads, w_out, preferred_element_type=jnp.float32)
    resid_group = embedded + jnp.sum(lax.all_gather(attn_part, "seq", axis=0, tiled=False), axis=0)
    resid_share = lax.dynamic_slice_in_dim(resid_group, seq_index * share, share, 0)
    moe_in = lax.all_gather(
        rms_scale(resid_group, moe_gain).astype(jnp.bfloat16), "exp", axis=0, tiled=True
    )
    router = jax.nn.sigmoid(jnp.dot(moe_in, w_router, preferred_element_type=jnp.float32))
    expert_count = w_router.shape[1]
    chosen_ids = grouped(expert_ids)
    picked = chosen_ids[:, :, None] == jnp.arange(expert_count, dtype=jnp.int32)[None, None, :]
    chosen = jnp.sum(jnp.where(picked, router[:, None, :], 0.0), axis=2)
    gate_weights = chosen / jnp.sum(chosen, axis=1, keepdims=True)
    rows_here = gate_pieces.shape[0]
    row_expert = (owner_index * rows_here + jnp.arange(rows_here, dtype=jnp.int32)) // PIECES
    token_weight = jnp.sum(
        jnp.where(
            chosen_ids[None, :, :] == row_expert[:, None, None], gate_weights[None, :, :], 0.0
        ),
        axis=2,
    )
    gate_out = jnp.einsum("nd,jdf->jnf", moe_in, gate_pieces, preferred_element_type=jnp.float32)
    up_out = jnp.einsum("nd,jdf->jnf", moe_in, up_pieces, preferred_element_type=jnp.float32)
    weighted_hidden = (jax.nn.silu(gate_out) * up_out * token_weight[:, :, None]).astype(
        jnp.bfloat16
    )
    routed = jnp.einsum(
        "jnf,jfd->nd", weighted_hidden, down_pieces, preferred_element_type=jnp.float32
    )
    share_count = tokens // n_seq
    share_start = seq_index * share_count
    share_rows = lax.dynamic_slice_in_dim(moe_in, share_start, share_count, 0)
    shared_hidden = (
        jax.nn.silu(jnp.dot(share_rows, shared_gate, preferred_element_type=jnp.float32))
        * jnp.dot(share_rows, shared_up, preferred_element_type=jnp.float32)
    ).astype(jnp.bfloat16)
    shared_out = jnp.dot(shared_hidden, shared_down, preferred_element_type=jnp.float32)
    term_rows = lax.dynamic_update_slice_in_dim(
        routed,
        lax.dynamic_slice_in_dim(routed, share_start, share_count, 0) + shared_out,
        share_start,
        0,
    )
    term_rows = jnp.swapaxes(term_rows.reshape(n_exp, n_seq, share, width), 0, 1)
    term_sum = jnp.sum(
        lax.all_to_all(
            term_rows.reshape(n_dev, share, width).astype(jnp.bfloat16),
            ("seq", "exp"),
            0,
            0,
            tiled=True,
        ).astype(jnp.float32),
        axis=0,
    )
    final_share = resid_share + term_sum
    norms_share = jnp.sqrt(jnp.mean(final_share * final_share, axis=-1))
    head_in = gather_all(rms_scale(final_share, final_gain).astype(jnp.bfloat16)).reshape(
        tokens, width
    )
    local_best = jnp.max(jnp.dot(head_in, w_head, preferred_element_type=jnp.float32), axis=-1)
    message = jnp.concatenate([local_best, norms_share], axis=0)
    heard = lax.all_to_all(
        jnp.broadcast_to(message[None, :], (n_dev, message.shape[0])),
        ("seq", "exp"),
        0,
        0,
        tiled=True,
    )
    greatest_logits = natural(jnp.max(heard[:, :tokens], axis=0))
    hidden_norms = natural(heard[:, tokens:].reshape(tokens))
    return (hidden_norms, greatest_logits)


def solution(mesh):
    in_specs = (
        P(),
        P(),
        P(),
        P(),
        P(("seq", "exp"), None),
        P(),
        P(None, "seq"),
        P(None, "seq"),
        P(None, "seq"),
        P("seq", None),
        P("exp", "seq", None),
        P("exp", "seq", None),
        P(),
        P(),
        P(("seq", "exp"), None, None),
        P(("seq", "exp"), None, None),
        P(("seq", "exp"), None, None),
        P(None, "exp"),
        P(None, "exp"),
        P("exp", None),
        P(),
        P(None, ("seq", "exp")),
    )
    out_specs = (P(), P())
    return jax.shard_map(
        on_device, mesh=mesh, in_specs=in_specs, out_specs=out_specs, check_vma=False
    )
```

profile of v0, /device:TPU:0, one launch (start us, length us, event | category | flops | bytes accessed | tf_op | source)
XLA Modules:
  0.0 184.5 jit_solution(12790132844402433581)
XLA Ops:
  0.7 0.8 subtract_clamp_fusion
  1.6 0.7 compare_and_fusion.2
  2.4 5.1 %gather_fusion = bf16[128,2048]{1,0:T(8,128)(2,1)S(1)} fusion(bf16[1600,2048]{1,0:T(8,128)(2,1)} %param.26, s32[1024]{0:T(1024)S(1)} %pad_clamp_fusion), kind=kCustom, calls=%fused_computation | custom fusion | bytes 1049088 | tf_op jit(solution)/shard_map/jit(_take)/gather | solution.py:88
  7.9 1.2 select_select_fusion
  9.1 6.3 %all-to-all-start = ((bf16[8,4,4,2048]{3,2,1,0:T(4,128)(2,1)}), bf16[8,4,4,2048]{3,2,1,0:T(4,128)(2,1)S(1)}, u32[]{:S(2)}, u32[]{:S(2)}) async-start(bf16[8,4,4,2048]{3,2,1,0:T(4,128)(2,1)} %select_select_fusion), calls=%async_computation | async-start | bytes 1048576 | tf_op jit(solution)/shard_map/all_to_all | solution.py:90
  15.5 0.8 dynamic-slice_compare_fusion
  16.3 4.0 %copy.166 = bf16[512,2048]{1,0:T(8,128)(2,1)} copy(bf16[512,2048]{0,1:T(8,128)(2,1)} %bitcast.153) | data formatting | bytes 4194304 | tf_op jit(solution)/shard_map/dot_general | solution.py:100
  20.3 3.9 %copy.167 = bf16[512,2048]{1,0:T(8,128)(2,1)} copy(bf16[512,2048]{0,1:T(8,128)(2,1)} %bitcast.154) | data formatting | bytes 4194304 | tf_op jit(solution)/shard_map/dot_general | solution.py:100
  24.3 4.0 %copy.168 = bf16[512,2048]{1,0:T(8,128)(2,1)} copy(bf16[512,2048]{0,1:T(8,128)(2,1)} %bitcast.155) | data formatting | bytes 4194304 | tf_op jit(solution)/shard_map/dot_general | solution.py:100
  29.0 1.8 all-to-all-done
  31.1 9.0 %all-gather = bf16[16,4,2048]{2,1,0:T(4,128)(2,1)S(1)} all-gather(bf16[4,4,2048]{2,1,0:T(4,128)(2,1)S(1)} %reduce_sum.137), channel_id=2, replica_groups=mesh['seq'=4,'exp'=8] {'seq'}, dimensions={0}, use_global_device_ids=true | all-gather | bytes 327680 | tf_op jit(solution)/shard_map/all_gather | solution.py:92
  40.5 2.4 %fusion.72 = f32[16,4,128]{2,0,1:T(8,128)S(1)} fusion(bf16[16,2048,1]{1,0,2:T(8,128)(2,1)S(1)} %reshape.577, bf16[4,128,2048]{2,1,0:T(8,128)(2,1)} %bitcast.151), kind=kOutput, calls=%fused_computation.132 | convolution fusion | flops 33554432 | bytes 2195456 | tf_op jit(solution)/shard_map/dot_general | solution.py:100
  44.2 2.2 %convolution_convert_fusion = bf16[16,4,128]{2,0,1:T(8,128)(2,1)S(1)} fusion(bf16[16,2048,1]{1,0,2:T(8,128)(2,1)S(1)} %reshape.577, bf16[4,128,2048]{2,1,0:T(8,128)(2,1)} %bitcast.149), kind=kOutput, calls=%fused_computation.31 | convolution fusion | flops 33562624 | bytes 2179072 | tf_op jit(solution)/shard_map/dot_general | solution.py:100
  46.6 8.8 %all-gather.1 = bf16[12,16,4,128]{3,1,2,0:T(8,128)(2,1)S(1)} all-gather(bf16[3,16,4,128]{3,1,2,0:T(8,128)(2,1)S(1)} %pad_maximum_fusion), channel_id=3, replica_groups=mesh['seq'=4,'exp'=8] {'seq'}, dimensions={0}, use_global_device_ids=true | all-gather | bytes 245760 | tf_op jit(solution)/shard_map/all_gather | solution.py:107
  55.5 3.5 %select_reduce_fusion = (f32[4,4,16]{0,2,1:T(8,128)S(1)}, f32[4,4,16,256]{3,0,2,1:T(4,128)S(1)}) fusion(pred[4,256]{1,0:T(4,128)(4,1)S(1)} %compare_and_fusion.1, bf16[4,4,16,128]{3,2,1,0:T(8,128)(2,1)S(1)} %bitcast.185, bf16[4,256,2048]{2,1,0:T(8,128)(2,1)} %param.32), kind=kOutput, calls=%fused_computation.39 | convolution fusion | flops 16973568 | bytes 4524032 | tf_op jit(solution)/shard_map/trhd,rphd->trhp/dot_general | solution.py:126
  59.6 2.9 %fusion = f32[4,16,4,128]{3,2,1,0:T(4,128)S(1)} fusion(f32[4,4,16,256]{3,0,2,1:T(4,128)S(1)} %get-tuple-element.22, f32[4,4,16]{0,2,1:T(8,128)S(1)} %get-tuple-element.21, pred[4,256]{1,0:T(4,128)(4,1)S(1)} %compare_and_fusion.1, bf16[4,256,2048]{2,1,0:T(8,128)(2,1)} %param.33), kind=kOutput, calls=%fused_computation.1 | convolution fusion | flops 16973824 | bytes 4589568 | tf_op jit(solution)/shard_map/trhp,rphd->trhd/dot_general | solution.py:132
  63.0 0.8 copy.149
  63.8 3.3 %all-to-all-start.1 = ((f32[4,1,8320]{2,1,0:T(1,128)}), f32[4,1,8320]{2,1,0:T(1,128)S(1)}, u32[]{:S(2)}, u32[]{:S(2)}) async-start(f32[4,1,8320]{2,1,0:T(1,128)} %copy.149), calls=%async_computation.1 | async-start | bytes 266240 | tf_op jit(solution)/shard_map/all_to_all | solution.py:149
  67.2 4.9 %all-to-all-done.1 = f32[4,1,8320]{2,1,0:T(1,128)S(1)} async-done(((f32[4,1,8320]{2,1,0:T(1,128)}), f32[4,1,8320]{2,1,0:T(1,128)S(1)}, u32[]{:S(2)}, u32[]{:S(2)}) %all-to-all-start.1) | async-done | bytes 133152 | tf_op jit(solution)/shard_map/all_to_all | solution.py:149
  74.0 9.4 %all-gather.2 = f32[64,2048]{1,0:T(8,128)S(1)} all-gather(f32[16,2048]{1,0:T(8,128)S(1)} %fusion.50), channel_id=4, replica_groups=mesh['seq'=4,'exp'=8] {'seq'}, dimensions={0}, use_global_device_ids=true | all-gather | bytes 655360 | tf_op jit(solution)/shard_map/all_gather | solution.py:181
  83.7 15.0 %all_gather.39 = bf16[128,2048]{1,0:T(8,128)(2,1)S(1)} all-gather(bf16[16,2048]{1,0:T(8,128)(2,1)S(1)} %multiply_convert_fusion), channel_id=1, replica_groups=mesh['seq'=4,'exp'=8] {'exp'}, dimensions={0}, use_global_device_ids=true | all-gather | bytes 589824 | tf_op jit(solution)/shard_map/all_gather | solution.py:183
  99.0 6.1 %convolution_bitcast_fusion.2 = f32[8,128,352]{1,2,0:T(8,128)S(1)} fusion(bf16[8,2048,352]{1,2,0:T(8,128)(2,1)} %param.36, bf16[128,2048]{1,0:T(8,128)(2,1)S(1)} %all_gather.39), kind=kOutput, calls=%fused_computation.11 | convolution fusion | flops 1476395008 | bytes 13500416 | tf_op jit(solution)/shard_map/nd,jdf->jnf/dot_general | solution.py:200
  105.9 14.7 %convolution_bitcast_fusion = f32[128,2048]{1,0:T(8,128)S(1)} fusion(bf16[8,352,2048]{2,1,0:T(8,128)(2,1)} %param.38, bf16[8,2048,352]{1,2,0:T(8,128)(2,1)} %param.37, f32[8,128,352]{1,2,0:T(8,128)S(1)} %convolution_bitcast_fusion.2, f32[8,128]{1,0:T(8,128)S(1)} %select_reduce_fusion.4, bf16[128,2048]{1,0:T(8,128)(2,1)S(1)} %all_gather.39), kind=kOutput, calls=%fused_computation.7 | convolution fusion | flops 2955313152 | bytes 26087424 | tf_op jit(solution)/shard_map/jnf,jfd->nd/dot_general | solution.py:205
  120.6 2.9 %fusion.6 = f32[128,2048]{1,0:T(8,128)S(1)} fusion(f32[128,2048]{1,0:T(8,128)S(1)} %convolution_bitcast_fusion, s32[]{:T(128)S(6)} %select_n.84, bf16[352,2048]{1,0:T(8,128)(2,1)} %param.41, bf16[2048,352]{0,1:T(8,128)(2,1)} %param.40, bf16[128,2048]{1,0:T(8,128)(2,1)S(1)} %all_gather.39, f32[32,352]{1,0:T(8,128)S(1)} %fusion.37), kind=kOutput, calls=%fused_computation.9 | convolution fusion | flops 92407808 | bytes 3589120 | tf_op jit(solution)/shard_map/dot_general | solution.py:215
  124.1 1.2 copy.164
  125.3 3.3 %all-to-all-start.2 = ((bf16[32,4,2048]{2,1,0:T(4,128)(2,1)}), bf16[32,4,2048]{2,1,0:T(4,128)(2,1)S(1)}, u32[]{:S(2)}, u32[]{:S(2)}) async-start(bf16[32,4,2048]{2,1,0:T(4,128)(2,1)} %copy.164), calls=%async_computation.2 | async-start | bytes 1048576 | tf_op jit(solution)/shard_map/all_to_all | solution.py:224
  128.6 16.4 %all-to-all-done.2 = bf16[32,4,2048]{2,1,0:T(4,128)(2,1)S(1)} async-done(((bf16[32,4,2048]{2,1,0:T(4,128)(2,1)}), bf16[32,4,2048]{2,1,0:T(4,128)(2,1)S(1)}, u32[]{:S(2)}, u32[]{:S(2)}) %all-to-all-start.2) | async-done | bytes 524320 | tf_op jit(solution)/shard_map/all_to_all | solution.py:224
  145.4 14.0 %all-gather.5 = bf16[8,4,2048]{2,1,0:T(4,128)(2,1)S(1)} all-gather(bf16[1,4,2048]{2,1,0:T(4,128)(2,1)S(1)} %fusion.49), channel_id=5, replica_groups=mesh['seq'=4,'exp'=8] {'exp'}, dimensions={0}, use_global_device_ids=true | all-gather | bytes 147456 | tf_op jit(solution)/shard_map/all_gather | solution.py:33
  159.3 9.4 %all-gather.4 = bf16[32,4,2048]{2,1,0:T(4,128)(2,1)S(1)} all-gather(bf16[8,4,2048]{2,1,0:T(4,128)(2,1)S(1)} %all-gather.5), channel_id=6, replica_groups=mesh['seq'=4,'exp'=8] {'seq'}, dimensions={0}, use_global_device_ids=true | all-gather | bytes 655360 | tf_op jit(solution)/shard_map/all_gather | solution.py:34
  168.9 4.9 %convolution_reduce_fusion = f32[128]{0:T(128)S(1)} fusion(bf16[128,2048]{1,0:T(8,128)(2,1)S(1)} %reshape.556, bf16[2048,1600]{0,1:T(8,128)(2,1)} %param.43), kind=kOutput, calls=%fused_computation.15 | convolution fusion | flops 839065472 | bytes 7078400 | tf_op jit(solution)/shard_map/dot_general | solution.py:238
  173.8 9.3 %all_to_all.31 = f32[32,1,132]{2,1,0:T(1,128)S(1)} all-to-all(f32[32,1,132]{2,1,0:T(1,128)S(1)} %broadcast_in_dim.145), channel_id=1, replica_groups=mesh['seq'=4,'exp'=8] {'seq','exp'}, dimensions={0} | all-to-all | bytes 33792 | tf_op jit(solution)/shard_map/all_to_all | solution.py:240
  183.8 0.7 reshape_reshape.3
  (113 shorter events, 9.5 us)
Async XLA Ops:
  0.6 72.9 %copy-start = (bf16[512,2048]{1,0:T(8,128)(2,1)S(1)}, bf16[512,2048]{1,0:T(8,128)(2,1)}, u32[]{:S(2)}) copy-start(bf16[512,2048]{1,0:T(8,128)(2,1)} %param.31) | copy-start | bytes 6291460
  7.6 7.9 %copy-start.9 = (s32[32]{0:T(128)S(1)}, s32[32]{0:T(128)}, u32[]{:S(2)}) copy-start(s32[32]{0:T(128)} %param.23) | copy-start | bytes 388
  9.1 21.7 %all-to-all-start = ((bf16[8,4,4,2048]{3,2,1,0:T(4,128)(2,1)}), bf16[8,4,4,2048]{3,2,1,0:T(4,128)(2,1)S(1)}, u32[]{:S(2)}, u32[]{:S(2)}) async-start(bf16[8,4,4,2048]{3,2,1,0:T(4,128)(2,1)} %select_select_fusion), calls=%async_computation | async-start | bytes 1048576 | tf_op jit(solution)/shard_map/all_to_all | solution.py:90
  24.3 4.2 %copy-start.5 = (s32[4,32,6]{1,0,2:T(4,128)S(1)}, s32[4,32,6]{1,0,2:T(4,128)}, u32[]{:S(2)}) copy-start(s32[4,32,6]{1,0,2:T(4,128)} %param.25) | copy-start | bytes 9220
  28.3 12.1 %copy-start.6 = (f32[2048]{0:T(1024)S(1)}, f32[2048]{0:T(1024)}, u32[]{:S(2)}) copy-start(f32[2048]{0:T(1024)} %param.27) | copy-start | bytes 24580
  40.5 2.4 %copy-start.2 = (bf16[512,2048]{1,0:T(8,128)(2,1)S(1)}, bf16[512,2048]{1,0:T(8,128)(2,1)}, u32[]{:S(2)}) copy-start(bf16[512,2048]{1,0:T(8,128)(2,1)} %copy.167) | copy-start | bytes 6291460
  63.8 8.3 %all-to-all-start.1 = ((f32[4,1,8320]{2,1,0:T(1,128)}), f32[4,1,8320]{2,1,0:T(1,128)S(1)}, u32[]{:S(2)}, u32[]{:S(2)}) async-start(f32[4,1,8320]{2,1,0:T(1,128)} %copy.149), calls=%async_computation.1 | async-start | bytes 266240 | tf_op jit(solution)/shard_map/all_to_all | solution.py:149
  73.5 10.1 %copy-start.7 = (f32[2048]{0:T(1024)S(1)}, f32[2048]{0:T(1024)}, u32[]{:S(2)}) copy-start(f32[2048]{0:T(1024)} %param.34) | copy-start | bytes 24580
  73.6 25.2 %copy-start.4 = (bf16[2048,64]{0,1:T(8,128)(2,1)S(1)}, bf16[2048,64]{0,1:T(8,128)(2,1)}, u32[]{:S(2)}) copy-start(bf16[2048,64]{0,1:T(8,128)(2,1)} %param.35) | copy-start | bytes 786436
  99.0 6.3 %copy-start.3 = (bf16[2048,352]{0,1:T(8,128)(2,1)S(1)}, bf16[2048,352]{0,1:T(8,128)(2,1)}, u32[]{:S(2)}) copy-start(bf16[2048,352]{0,1:T(8,128)(2,1)} %param.39) | copy-start | bytes 4325380
  123.8 21.5 %copy-start.8 = (f32[2048]{0:T(1024)S(1)}, f32[2048]{0:T(1024)}, u32[]{:S(2)}) copy-start(f32[2048]{0:T(1024)} %param.42) | copy-start | bytes 24580
  125.3 19.6 %all-to-all-start.2 = ((bf16[32,4,2048]{2,1,0:T(4,128)(2,1)}), bf16[32,4,2048]{2,1,0:T(4,128)(2,1)S(1)}, u32[]{:S(2)}, u32[]{:S(2)}) async-start(bf16[32,4,2048]{2,1,0:T(4,128)(2,1)} %copy.164), calls=%async_computation.2 | async-start | bytes 1048576 | tf_op jit(solution)/shard_map/all_to_all | solution.py:224
  168.8 15.6 %copy-start.1 = (bf16[512,2048]{1,0:T(8,128)(2,1)S(1)}, bf16[512,2048]{1,0:T(8,128)(2,1)}, u32[]{:S(2)}) copy-start(bf16[512,2048]{1,0:T(8,128)(2,1)} %param.31) | copy-start | bytes 6291460
where the time goes:
time: 185 us; the launch traced here: 184 us
  blocking collectives  75 us (41%)
  matrix products  42 us (23%)
  local copies, waits for them, and re-layouts  24.2 us (13%)
  waiting for transfers between devices  23.1 us (12%)
  starting transfers between devices  12.9 us (7%)
  other arithmetic  6.12 us (3%)
    all_to_all x1, waiting for transfers between devices, on_device(): lax.all_to_all(term_rows.reshape(n_dev, share, width).astype(jnp.bfloat16...  16.4 us
    all_gather x1, blocking collectives, on_device(): lax.all_gather(rms_scale(resid_group, moe_gain).astype(jnp.bfloat16), 'ex...  15 us
    dot_general x1, matrix products, on_device(): jnp.einsum('jnf,jfd->nd', weighted_hidden, down_pieces, preferred_element...  14.7 us
    all_gather x1, blocking collectives, gather_all(): inner = lax.all_gather(values, 'exp', axis=0, tiled=False)  14 us
    dot_general x3, local copies, waits for them, and re-layouts, project(): jnp.dot(attn_in, weight, preferred_element_type=jnp.float32)  11.9 us
    all_gather x1, blocking collectives, on_device(): lax.all_gather(attn_part, 'seq', axis=0, tiled=False)  9.45 us
    all_gather x1, blocking collectives, gather_all(): return lax.all_gather(inner, 'seq', axis=0, tiled=False)  9.37 us
    all_to_all x1, blocking collectives, on_device(): lax.all_to_all(jnp.broadcast_to(message[None, :], (n_dev, message.shape[0...  9.32 us
  transfers between devices with their start and end apart: 3, of which 3 were waited for; matrix products, arithmetic and copies ran while one was open for 7% of the time, Pallas kernels for 0%

commit v1 on v0

--- a/solution.py
+++ b/solution.py
@@ -9,6 +9,17 @@
 BLK = 16
 epsilon = 1e-06
 negative = -1e30
+
+
+def in_blocks(x, dim, size):
+    before, after = (x.shape[:dim], x.shape[dim + 1 :])
+    return jnp.moveaxis(x.reshape(*before, size, -1, *after), dim, 0)
+
+
+def laid_out(blocks, dim):
+    blocks = jnp.moveaxis(blocks, 0, dim)
+    shape = blocks.shape
+    return blocks.reshape(*shape[:dim], shape[dim] * shape[dim + 1], *shape[dim + 2 :])
 
 
 def rms_scale(values, scales):
@@ -146,7 +157,14 @@
     packed = jnp.concatenate(
         [by_owner(local_mixture), by_owner(local_top), by_owner(local_totals)], axis=1
     )
-    got = lax.all_to_all(packed, "seq", 0, 0, tiled=True)
+    size, mine = (lax.axis_size("seq"), lax.axis_index("seq"))
+    tiles = in_blocks(packed, 0, size)
+    gathered = [tiles[mine]]
+    for step in range(1, size):
+        sent = tiles[mine ^ step]
+        gathered.append(lax.ppermute(sent, "seq", [(i, i ^ step) for i in range(size)]))
+    tiles = jnp.stack(gathered)[mine ^ jnp.arange(size)]
+    got = laid_out(tiles, 0)
     got_mixture = got[:, :mix_len].reshape(n_seq, steps, own_count, heads_here, HDIM)
     got_top = got[:, mix_len : mix_len + stat_len].reshape(n_seq, steps, own_count, heads_here)
     got_totals = got[:, mix_len + stat_len :].reshape(n_seq, steps, own_count, heads_here)

time: 185 us -> 182 us (0.984)
  waiting for transfers between devices: 23.1 us -> 20.9 us
    all_to_all x1 -> x0, waiting for transfers between devices: 4.95 us -> none  [on_device(): got = lax.all_to_all(packed, 'seq', 0, 0, tiled=True)]
    ppermute x0 -> x3, starting transfers between devices: none -> 3.55 us  [on_device(): lax.ppermute(sent, 'seq', [(i, i ^ step) for i in range(size)])]
    all_to_all x1 -> x0, starting transfers between devices: 3.32 us -> none  [on_device(): got = lax.all_to_all(packed, 'seq', 0, 0, tiled=True)]
    ppermute x0 -> x3, waiting for transfers between devices: none -> 2.81 us  [on_device(): lax.ppermute(sent, 'seq', [(i, i ^ step) for i in range(size)])]
  transfers between devices with their start and end apart: 3 -> 5, of which waited for: 3 -> 4; matrix products, arithmetic and copies ran while one was open for 7% -> 8% of each run, Pallas kernels for 0% -> 0%
where the time goes in v1:
time: 182 us; the launch traced here: 181 us
  blocking collectives  74.6 us (41%)
  matrix products  40.4 us (22%)
  local copies, waits for them, and re-layouts  24.2 us (13%)
  waiting for transfers between devices  20.9 us (11%)
  starting transfers between devices  13.4 us (7%)
  other arithmetic  6.26 us (3%)
    all_to_all x1, waiting for transfers between devices, on_device(): lax.all_to_all(term_rows.reshape(n_dev, share, width).astype(jnp.bfloat16...  16.4 us
    all_gather x1, blocking collectives, on_device(): lax.all_gather(rms_scale(resid_group, moe_gain).astype(jnp.bfloat16), 'ex...  15.1 us
    dot_general x1, matrix products, on_device(): jnp.einsum('jnf,jfd->nd', weighted_hidden, down_pieces, preferred_element...  14.7 us
    all_gather x1, blocking collectives, gather_all(): inner = lax.all_gather(values, 'exp', axis=0, tiled=False)  14 us
    dot_general x3, local copies, waits for them, and re-layouts, project(): jnp.dot(attn_in, weight, preferred_element_type=jnp.float32)  11.9 us
    all_gather x1, blocking collectives, gather_all(): return lax.all_gather(inner, 'seq', axis=0, tiled=False)  9.37 us
    all_to_all x1, blocking collectives, on_device(): lax.all_to_all(jnp.broadcast_to(message[None, :], (n_dev, message.shape[0...  9.33 us
    all_gather x1, blocking collectives, on_device(): row_parts = lax.all_gather(row_part, 'seq', axis=0, tiled=False)  9 us
  transfers between devices with their start and end apart: 5, of which 4 were waited for; matrix products, arithmetic and copies ran while one was open for 8% of the time, Pallas kernels for 0%

profile of v1, /device:TPU:0, one launch (start us, length us, event | category | flops | bytes accessed | tf_op | source)
XLA Modules:
  0.0 180.8 jit_solution(12248574632453905633)
XLA Ops:
  0.7 0.8 subtract_clamp_fusion
  1.6 0.7 compare_and_fusion.2
  2.4 5.1 %gather_fusion = bf16[128,2048]{1,0:T(8,128)(2,1)S(1)} fusion(bf16[1600,2048]{1,0:T(8,128)(2,1)} %param.26, s32[1024]{0:T(1024)S(1)} %pad_clamp_fusion.1), kind=kCustom, calls=%fused_computation | custom fusion | bytes 1049088 | tf_op jit(solution)/shard_map/jit(_take)/gather | solution.py:99
  7.9 1.2 select_select_fusion
  9.1 6.3 %all-to-all-start = ((bf16[8,4,4,2048]{3,2,1,0:T(4,128)(2,1)}), bf16[8,4,4,2048]{3,2,1,0:T(4,128)(2,1)S(1)}, u32[]{:S(2)}, u32[]{:S(2)}) async-start(bf16[8,4,4,2048]{3,2,1,0:T(4,128)(2,1)} %select_select_fusion), calls=%async_computation | async-start | bytes 1048576 | tf_op jit(solution)/shard_map/all_to_all | solution.py:101
  15.6 0.8 dynamic-slice_compare_fusion
  16.4 4.0 %copy.164 = bf16[512,2048]{1,0:T(8,128)(2,1)} copy(bf16[512,2048]{0,1:T(8,128)(2,1)} %bitcast.158) | data formatting | bytes 4194304 | tf_op jit(solution)/shard_map/dot_general | solution.py:111
  20.3 3.9 %copy.165 = bf16[512,2048]{1,0:T(8,128)(2,1)} copy(bf16[512,2048]{0,1:T(8,128)(2,1)} %bitcast.159) | data formatting | bytes 4194304 | tf_op jit(solution)/shard_map/dot_general | solution.py:111
  24.3 4.0 %copy.166 = bf16[512,2048]{1,0:T(8,128)(2,1)} copy(bf16[512,2048]{0,1:T(8,128)(2,1)} %bitcast.160) | data formatting | bytes 4194304 | tf_op jit(solution)/shard_map/dot_general | solution.py:111
  29.1 1.7 all-to-all-done
  31.1 9.0 %all-gather = bf16[16,4,2048]{2,1,0:T(4,128)(2,1)S(1)} all-gather(bf16[4,4,2048]{2,1,0:T(4,128)(2,1)S(1)} %reduce_sum.137), channel_id=2, replica_groups=mesh['seq'=4,'exp'=8] {'seq'}, dimensions={0}, use_global_device_ids=true | all-gather | bytes 327680 | tf_op jit(solution)/shard_map/all_gather | solution.py:103
  40.5 2.4 %fusion.73 = f32[16,4,128]{2,0,1:T(8,128)S(1)} fusion(bf16[16,2048,1]{1,0,2:T(8,128)(2,1)S(1)} %reshape.614, bf16[4,128,2048]{2,1,0:T(8,128)(2,1)} %bitcast.156), kind=kOutput, calls=%fused_computation.140 | convolution fusion | flops 33554432 | bytes 2195456 | tf_op jit(solution)/shard_map/dot_general | solution.py:111
  42.9 0.7 fusion.74
  44.5 8.8 %all-gather.1 = bf16[12,16,4,128]{3,1,2,0:T(8,128)(2,1)S(1)} all-gather(bf16[3,16,4,128]{3,1,2,0:T(8,128)(2,1)S(1)} %pad_maximum_fusion), channel_id=3, replica_groups=mesh['seq'=4,'exp'=8] {'seq'}, dimensions={0}, use_global_device_ids=true | all-gather | bytes 245760 | tf_op jit(solution)/shard_map/all_gather | solution.py:118
  53.4 3.5 %select_reduce_fusion = (f32[4,4,16]{0,2,1:T(8,128)S(1)}, f32[4,4,16,256]{3,0,2,1:T(4,128)S(1)}) fusion(pred[4,256]{1,0:T(4,128)(4,1)S(1)} %compare_and_fusion.1, bf16[4,4,16,128]{3,2,1,0:T(8,128)(2,1)S(1)} %bitcast.186, bf16[4,256,2048]{2,1,0:T(8,128)(2,1)} %param.32), kind=kOutput, calls=%fused_computation.40 | convolution fusion | flops 16973568 | bytes 4524032 | tf_op jit(solution)/shard_map/trhd,rphd->trhp/dot_general | solution.py:137
  57.5 2.9 %fusion = f32[4,16,4,128]{3,2,1,0:T(4,128)S(1)} fusion(f32[4,4,16,256]{3,0,2,1:T(4,128)S(1)} %get-tuple-element.26, f32[4,4,16]{0,2,1:T(8,128)S(1)} %get-tuple-element.25, pred[4,256]{1,0:T(4,128)(4,1)S(1)} %compare_and_fusion.1, bf16[4,256,2048]{2,1,0:T(8,128)(2,1)} %param.33), kind=kOutput, calls=%fused_computation.2 | convolution fusion | flops 16973824 | bytes 4589568 | tf_op jit(solution)/shard_map/trhp,rphd->trhd/dot_general | solution.py:143
  61.5 1.6 collective-permute-start.1
  63.2 1.5 collective-permute-start.2
  65.5 2.5 %collective-permute-done.2 = f32[1,8320]{1,0:T(1,128)S(1)} collective-permute-done((f32[1,8320]{1,0:T(1,128)S(1)}, f32[1,8320]{1,0:T(1,128)S(1)}, u32[]{:S(2)}, u32[]{:S(2)}) %collective-permute-start.2) | collective-permute-done | bytes 33312 | tf_op jit(solution)/shard_map/ppermute | solution.py:165
  70.5 8.9 %all-gather.2 = f32[64,2048]{1,0:T(8,128)S(1)} all-gather(f32[16,2048]{1,0:T(8,128)S(1)} %fusion.50), channel_id=4, replica_groups=mesh['seq'=4,'exp'=8] {'seq'}, dimensions={0}, use_global_device_ids=true | all-gather | bytes 655360 | tf_op jit(solution)/shard_map/all_gather | solution.py:199
  79.7 15.1 %all_gather.39 = bf16[128,2048]{1,0:T(8,128)(2,1)S(1)} all-gather(bf16[16,2048]{1,0:T(8,128)(2,1)S(1)} %multiply_convert_fusion), channel_id=1, replica_groups=mesh['seq'=4,'exp'=8] {'exp'}, dimensions={0}, use_global_device_ids=true | all-gather | bytes 589824 | tf_op jit(solution)/shard_map/all_gather | solution.py:201
  95.2 6.1 %convolution_bitcast_fusion.2 = f32[8,128,352]{1,2,0:T(8,128)S(1)} fusion(bf16[8,2048,352]{1,2,0:T(8,128)(2,1)} %param.36, bf16[128,2048]{1,0:T(8,128)(2,1)S(1)} %all_gather.39), kind=kOutput, calls=%fused_computation.12 | convolution fusion | flops 1476395008 | bytes 13500416 | tf_op jit(solution)/shard_map/nd,jdf->jnf/dot_general | solution.py:218
  102.0 14.7 %convolution_bitcast_fusion = f32[128,2048]{1,0:T(8,128)S(1)} fusion(bf16[8,352,2048]{2,1,0:T(8,128)(2,1)} %param.38, bf16[8,2048,352]{1,2,0:T(8,128)(2,1)} %param.37, f32[8,128,352]{1,2,0:T(8,128)S(1)} %convolution_bitcast_fusion.2, f32[8,128]{1,0:T(8,128)S(1)} %select_reduce_fusion.4, bf16[128,2048]{1,0:T(8,128)(2,1)S(1)} %all_gather.39), kind=kOutput, calls=%fused_computation.8 | convolution fusion | flops 2955313152 | bytes 26087424 | tf_op jit(solution)/shard_map/jnf,jfd->nd/dot_general | solution.py:223
  116.7 2.9 %fusion.6 = f32[128,2048]{1,0:T(8,128)S(1)} fusion(f32[128,2048]{1,0:T(8,128)S(1)} %convolution_bitcast_fusion, s32[]{:T(128)S(6)} %select_n.111, bf16[352,2048]{1,0:T(8,128)(2,1)} %param.41, bf16[2048,352]{0,1:T(8,128)(2,1)} %param.40, bf16[128,2048]{1,0:T(8,128)(2,1)S(1)} %all_gather.39, f32[32,352]{1,0:T(8,128)S(1)} %fusion.37), kind=kOutput, calls=%fused_computation.10 | convolution fusion | flops 92407808 | bytes 3589120 | tf_op jit(solution)/shard_map/dot_general | solution.py:233
  120.2 1.2 copy.162
  121.4 3.5 %all-to-all-start.1 = ((bf16[32,4,2048]{2,1,0:T(4,128)(2,1)}), bf16[32,4,2048]{2,1,0:T(4,128)(2,1)S(1)}, u32[]{:S(2)}, u32[]{:S(2)}) async-start(bf16[32,4,2048]{2,1,0:T(4,128)(2,1)} %copy.162), calls=%async_computation.1 | async-start | bytes 1048576 | tf_op jit(solution)/shard_map/all_to_all | solution.py:242
  124.9 16.4 %all-to-all-done.1 = bf16[32,4,2048]{2,1,0:T(4,128)(2,1)S(1)} async-done(((bf16[32,4,2048]{2,1,0:T(4,128)(2,1)}), bf16[32,4,2048]{2,1,0:T(4,128)(2,1)S(1)}, u32[]{:S(2)}, u32[]{:S(2)}) %all-to-all-start.1) | async-done | bytes 524320 | tf_op jit(solution)/shard_map/all_to_all | solution.py:242
  141.7 14.0 %all-gather.5 = bf16[8,4,2048]{2,1,0:T(4,128)(2,1)S(1)} all-gather(bf16[1,4,2048]{2,1,0:T(4,128)(2,1)S(1)} %fusion.49), channel_id=5, replica_groups=mesh['seq'=4,'exp'=8] {'exp'}, dimensions={0}, use_global_device_ids=true | all-gather | bytes 147456 | tf_op jit(solution)/shard_map/all_gather | solution.py:44
  155.7 9.4 %all-gather.4 = bf16[32,4,2048]{2,1,0:T(4,128)(2,1)S(1)} all-gather(bf16[8,4,2048]{2,1,0:T(4,128)(2,1)S(1)} %all-gather.5), channel_id=6, replica_groups=mesh['seq'=4,'exp'=8] {'seq'}, dimensions={0}, use_global_device_ids=true | all-gather | bytes 655360 | tf_op jit(solution)/shard_map/all_gather | solution.py:45
  165.2 4.9 %convolution_reduce_fusion = f32[128]{0:T(128)S(1)} fusion(bf16[128,2048]{1,0:T(8,128)(2,1)S(1)} %reshape.582, bf16[2048,1600]{0,1:T(8,128)(2,1)} %param.43), kind=kOutput, calls=%fused_computation.16 | convolution fusion | flops 839065472 | bytes 7078400 | tf_op jit(solution)/shard_map/dot_general | solution.py:256
  170.1 9.3 %all_to_all.19 = f32[32,1,132]{2,1,0:T(1,128)S(1)} all-to-all(f32[32,1,132]{2,1,0:T(1,128)S(1)} %broadcast_in_dim.146), channel_id=1, replica_groups=mesh['seq'=4,'exp'=8] {'seq','exp'}, dimensions={0} | all-to-all | bytes 33792 | tf_op jit(solution)/shard_map/all_to_all | solution.py:258
  180.2 0.7 reshape_reshape.3
  (122 shorter events, 11.1 us)
Async XLA Ops:
  0.6 69.5 %copy-start = (bf16[512,2048]{1,0:T(8,128)(2,1)S(1)}, bf16[512,2048]{1,0:T(8,128)(2,1)}, u32[]{:S(2)}) copy-start(bf16[512,2048]{1,0:T(8,128)(2,1)} %param.31) | copy-start | bytes 6291460
  7.6 7.9 %copy-start.10 = (s32[32]{0:T(128)S(1)}, s32[32]{0:T(128)}, u32[]{:S(2)}) copy-start(s32[32]{0:T(128)} %param.23) | copy-start | bytes 388
  9.1 21.7 %all-to-all-start = ((bf16[8,4,4,2048]{3,2,1,0:T(4,128)(2,1)}), bf16[8,4,4,2048]{3,2,1,0:T(4,128)(2,1)S(1)}, u32[]{:S(2)}, u32[]{:S(2)}) async-start(bf16[8,4,4,2048]{3,2,1,0:T(4,128)(2,1)} %select_select_fusion), calls=%async_computation | async-start | bytes 1048576 | tf_op jit(solution)/shard_map/all_to_all | solution.py:101
  24.3 4.2 %copy-start.6 = (s32[4,32,6]{1,0,2:T(4,128)S(1)}, s32[4,32,6]{1,0,2:T(4,128)}, u32[]{:S(2)}) copy-start(s32[4,32,6]{1,0,2:T(4,128)} %param.25) | copy-start | bytes 9220
  24.3 16.0 %copy-start.7 = (f32[2048]{0:T(1024)S(1)}, f32[2048]{0:T(1024)}, u32[]{:S(2)}) copy-start(f32[2048]{0:T(1024)} %param.27) | copy-start | bytes 24580
  40.5 2.4 %copy-start.3 = (bf16[512,2048]{1,0:T(8,128)(2,1)S(1)}, bf16[512,2048]{1,0:T(8,128)(2,1)}, u32[]{:S(2)}) copy-start(bf16[512,2048]{1,0:T(8,128)(2,1)} %copy.165) | copy-start | bytes 6291460
  40.5 3.2 %copy-start.2 = (bf16[512,2048]{1,0:T(8,128)(2,1)S(1)}, bf16[512,2048]{1,0:T(8,128)(2,1)}, u32[]{:S(2)}) copy-start(bf16[512,2048]{1,0:T(8,128)(2,1)} %copy.166) | copy-start | bytes 6291460
  61.1 4.1 %collective-permute-start = (f32[1,8320]{1,0:T(1,128)S(1)}, f32[1,8320]{1,0:T(1,128)S(1)}, u32[]{:S(2)}, u32[]{:S(2)}) collective-permute-start(f32[1,8320]{1,0:T(1,128)S(1)} %get-tuple-element.14), channel_id=1, source_target_pairs={{0,8},{8,0},{16,24},{24,16},{1,9},{9,1},{17,25},{25,17},{2,10},{10... | collective-permute-start | bytes 99848 | tf_op jit(solution)/shard_map/ppermute | solution.py:165
  61.5 3.9 %collective-permute-start.1 = (f32[1,8320]{1,0:T(1,128)S(1)}, f32[1,8320]{1,0:T(1,128)S(1)}, u32[]{:S(2)}, u32[]{:S(2)}) collective-permute-start(f32[1,8320]{1,0:T(1,128)S(1)} %get-tuple-element.13), channel_id=1, source_target_pairs={{0,16},{8,24},{16,0},{24,8},{1,17},{9,25},{17,1},{25,9},{2,18},{10... | collective-permute-start | bytes 99848 | tf_op jit(solution)/shard_map/ppermute | solution.py:165
  63.2 4.8 %collective-permute-start.2 = (f32[1,8320]{1,0:T(1,128)S(1)}, f32[1,8320]{1,0:T(1,128)S(1)}, u32[]{:S(2)}, u32[]{:S(2)}) collective-permute-start(f32[1,8320]{1,0:T(1,128)S(1)} %get-tuple-element.12), channel_id=1, source_target_pairs={{0,24},{8,16},{16,8},{24,0},{1,25},{9,17},{17,9},{25,1},{2,26},{10... | collective-permute-start | bytes 99848 | tf_op jit(solution)/shard_map/ppermute | solution.py:165
  70.1 9.6 %copy-start.8 = (f32[2048]{0:T(1024)S(1)}, f32[2048]{0:T(1024)}, u32[]{:S(2)}) copy-start(f32[2048]{0:T(1024)} %param.34) | copy-start | bytes 24580
  70.1 24.8 %copy-start.5 = (bf16[2048,64]{0,1:T(8,128)(2,1)S(1)}, bf16[2048,64]{0,1:T(8,128)(2,1)}, u32[]{:S(2)}) copy-start(bf16[2048,64]{0,1:T(8,128)(2,1)} %param.35) | copy-start | bytes 786436
  95.2 6.3 %copy-start.4 = (bf16[2048,352]{0,1:T(8,128)(2,1)S(1)}, bf16[2048,352]{0,1:T(8,128)(2,1)}, u32[]{:S(2)}) copy-start(bf16[2048,352]{0,1:T(8,128)(2,1)} %param.39) | copy-start | bytes 4325380
  119.9 21.7 %copy-start.9 = (f32[2048]{0:T(1024)S(1)}, f32[2048]{0:T(1024)}, u32[]{:S(2)}) copy-start(f32[2048]{0:T(1024)} %param.42) | copy-start | bytes 24580
  121.4 19.8 %all-to-all-start.1 = ((bf16[32,4,2048]{2,1,0:T(4,128)(2,1)}), bf16[32,4,2048]{2,1,0:T(4,128)(2,1)S(1)}, u32[]{:S(2)}, u32[]{:S(2)}) async-start(bf16[32,4,2048]{2,1,0:T(4,128)(2,1)} %copy.162), calls=%async_computation.1 | async-start | bytes 1048576 | tf_op jit(solution)/shard_map/all_to_all | solution.py:242
  165.2 15.6 %copy-start.1 = (bf16[512,2048]{1,0:T(8,128)(2,1)S(1)}, bf16[512,2048]{1,0:T(8,128)(2,1)}, u32[]{:S(2)}) copy-start(bf16[512,2048]{1,0:T(8,128)(2,1)} %param.31) | copy-start | bytes 6291460
